TPU v7x, 32 devices: a whole 2x2x4 slice. The times are simulated.
32 devices in a mesh: dp: 8 (over z, core), tensor: 4 (over y, x).
Axes of the slice: x: 2, y: 2, z: 4, core: 2. Of those that a mesh axis runs over, the one named last changes fastest.
Arguments:
- tokens: bfloat16 [512, 8192], P(None, 'dp'), may hold values from -6 to 6
- w_gate_up: bfloat16 [8192, 2, 28672], P('dp', None, 'tensor'), may hold values from -0.0625 to 0.0625
- w_down: bfloat16 [28672, 8192], P('tensor', 'dp'), may hold values from -0.03125 to 0.03125
- targets: bfloat16 [512, 8192], P(None, 'dp'), may hold values from -3 to 3
- proj_model: bfloat16 [8192, 128], P('dp'), may hold values from -0.0625 to 0.0625
- proj_hidden: bfloat16 [28672, 192], P('tensor'), may hold values from -0.03125 to 0.03125
- store: bfloat16 [4096, 12288], P(('dp', 'tensor')), may hold values from -0.017944336 to 0.017944336
Outputs:
- scores: float32 [4, 4096], P(None, ('dp', 'tensor'))
All inputs are finite; a program needn't handle non-finite values.
Results may differ from a plain program's by a relative error of at most 0.02.
Values may be sent and summed in bfloat16 or wider, within the bound.
No kernel may reach another device: no remote copies, remote signals or barrier semaphores. Data moves between devices by JAX's collectives and lax.ppermute only.
A program may use at most 256 MiB of HBM per device.

v0:
```python
import jax
import jax.numpy as jnp
from jax import lax
from jax.sharding import PartitionSpec as P

RANK = 64
SEQ = 128


def local(tokens, w_gate_up, w_down, targets, proj_model, proj_hidden, store):
    total = tokens.shape[0]
    hi = lax.Precision.HIGHEST
    tests = total // SEQ
    a_in_part = jnp.dot(tokens, proj_model[:, :RANK], preferred_element_type=jnp.float32)
    n_dp = lax.axis_size("dp")
    rows = total // n_dp
    width_ff = w_down.shape[0]
    both = jnp.einsum("td,dkf->ktf", tokens, w_gate_up, preferred_element_type=jnp.float32)
    both = both.astype(jnp.bfloat16).reshape(2, n_dp, rows, width_ff).transpose(1, 0, 2, 3)
    gate_up = (
        lax.psum_scatter(
            both.reshape(n_dp * 2 * rows, width_ff), "dp", scatter_dimension=0, tiled=True
        )
        .astype(jnp.float32)
        .reshape(2, rows, width_ff)
    )
    gate = gate_up[0]
    up = gate_up[1]
    sig = jax.nn.sigmoid(gate)
    act = gate * sig
    hidden = (act * up).astype(jnp.bfloat16)
    out_part = jnp.dot(
        lax.all_gather(hidden, "dp", axis=0, tiled=True), w_down, preferred_element_type=jnp.float32
    )
    out_full = lax.psum(out_part, "tensor")
    cot = (out_full - targets.astype(jnp.float32)).astype(jnp.bfloat16)
    a_out_part = jnp.dot(cot, proj_model[:, RANK:], preferred_element_type=jnp.float32)
    side = lax.psum(jnp.concatenate([a_in_part, a_out_part], axis=1), "dp")
    grad_hidden = lax.psum_scatter(
        lax.dot_general(cot, w_down, (((1,), (1,)), ((), ())), preferred_element_type=jnp.float32),
        "dp",
        scatter_dimension=0,
        tiled=True,
    )
    dgate = (grad_hidden * up * sig * (1.0 + gate * (1.0 - sig))).astype(jnp.bfloat16)
    dup = (grad_hidden * act).astype(jnp.bfloat16)
    hid_part = jnp.concatenate(
        [
            jnp.dot(dgate, proj_hidden[:, :RANK], preferred_element_type=jnp.float32),
            jnp.dot(dup, proj_hidden[:, RANK : 2 * RANK], preferred_element_type=jnp.float32),
            jnp.dot(hidden, proj_hidden[:, 2 * RANK :], preferred_element_type=jnp.float32),
        ],
        axis=1,
    )
    hid_sum = lax.all_gather(lax.psum(hid_part, "tensor"), "dp", axis=0, tiled=True)
    a_in = side[:, :RANK]
    a_out = side[:, RANK:]
    position = lax.iota(jnp.int32, total)
    member = ((position // SEQ)[:, None] == lax.iota(jnp.int32, tests)[None, :]).astype(jnp.float32)
    g_gate = jnp.einsum("ts,ti,tj->sij", member, a_in, hid_sum[:, :RANK], precision=hi)
    g_up = jnp.einsum("ts,ti,tj->sij", member, a_in, hid_sum[:, RANK : 2 * RANK], precision=hi)
    g_down = jnp.einsum("ts,ti,tj->sij", member, hid_sum[:, 2 * RANK :], a_out, precision=hi)
    grads = jnp.stack([g_gate, g_up, g_down], axis=1).reshape(tests, 3 * RANK * RANK)
    return lax.dot_general(
        grads.astype(jnp.bfloat16),
        store,
        (((1,), (1,)), ((), ())),
        preferred_element_type=jnp.float32,
    )


def solution(mesh):
    return jax.shard_map(
        local,
        mesh=mesh,
        in_specs=(
            P(None, "dp"),
            P("dp", None, "tensor"),
            P("tensor", "dp"),
            P(None, "dp"),
            P("dp", None),
            P("tensor", None),
            P(("dp", "tensor"), None),
        ),
        out_specs=P(None, ("dp", "tensor")),
        check_vma=False,
    )
```

profile of v0, /device:TPU:0, one launch (start us, length us, event | category | flops | bytes accessed | tf_op | source)
XLA Modules:
  0.0 616.4 jit_solution(7169694522479102521)
XLA Ops:
  6.5 0.0 copy-start
  6.5 0.0 reduce-scatter.3.cloned.1.call-start
  6.5 24.9 %fusion.2 = bf16[2,7168,512]{1,2,0:T(8,128)(2,1)} fusion(bf16[1024,2,7168]{2,1,0:T(2,128)(2,1)} %param.8, bf16[512,1024]{1,0:T(8,128)(2,1)} %param.7), kind=kOutput, calls=%fused_computation.2 | convolution fusion | flops 15039725568 | bytes 45088768 | tf_op jit(solution)/shard_map/td,dkf->ktf/dot_general | solution.py:18
  31.4 13.5 %copy.14 = bf16[8,2,64,7168]{3,2,1,0:T(8,128)(2,1)} copy(bf16[8,2,64,7168]{3,2,0,1:T(8,128)(2,1)} %bitcast.40) | data formatting | bytes 29360128 | tf_op jit(solution)/shard_map/transpose | solution.py:19
  44.9 0.0 reduce-scatter.3.cloned.1.call-update
  45.0 0.0 all-gather.2.cloned.1.call-start
  45.0 151.8 %reduce-scatter.3.cloned.1.call-done = bf16[128,7168]{1,0:T(8,128)(2,1)} async-done(((bf16[1024,7168]{1,0:T(8,128)(2,1)}), bf16[128,7168]{1,0:T(8,128)(2,1)}) %reduce-scatter.3.cloned.1.call-update) | async-done | bytes 1835024 | tf_op jit(solution)/shard_map/reduce_scatter | solution.py:21
  196.8 1.9 convert_element_type.31
  198.7 0.0 copy-start.1
  198.7 1.8 copy-done.1
  200.5 1.4 multiply_convert_fusion.2
  201.9 0.0 all-gather.2.cloned.1.call-update
  201.9 0.0 all-reduce.3.cloned.1.call-start
  202.0 71.8 %all-gather.2.cloned.1.call-done = bf16[512,7168]{1,0:T(8,128)(2,1)} async-done(((bf16[64,7168]{1,0:T(8,128)(2,1)}), bf16[512,7168]{1,0:T(8,128)(2,1)}) %all-gather.2.cloned.1.call-update) | async-done | bytes 7340048 | tf_op jit(solution)/shard_map/all_gather | solution.py:33
  273.8 14.3 %fusion.37 = f32[512,1024]{1,0:T(8,128)} fusion(bf16[512,7168]{1,0:T(8,128)(2,1)} %all-gather.2.cloned.1.call-done, bf16[7168,1024]{1,0:T(8,128)(2,1)} %param.9), kind=kOutput, calls=%fused_computation.53 | convolution fusion | flops 7516192768 | bytes 24117248 | tf_op jit(solution)/shard_map/dot_general | solution.py:32
  288.1 0.0 copy-start.3
  288.1 0.0 all-reduce.3.cloned.1.call-update
  288.1 0.0 all-reduce.5.cloned.1.call-start
  288.2 0.9 copy-done.3
  289.1 1.7 fusion.27
  290.7 65.8 %all-reduce.3.cloned.1.call-done = f32[512,1024]{1,0:T(8,128)} async-done(((f32[512,1024]{1,0:T(8,128)}), f32[512,1024]{1,0:T(8,128)}) %all-reduce.3.cloned.1.call-update) | async-done | bytes 2097168 | tf_op jit(solution)/shard_map/psum | solution.py:35
  356.5 2.4 fusion.25
  358.9 0.7 pad_maximum_fusion
  359.6 0.0 all-reduce.5.cloned.1.call-update
  359.7 0.2 reduce-scatter.5.cloned.1.call-start
  359.9 14.9 %fusion.36 = f32[512,7168]{1,0:T(8,128)} fusion(bf16[7168,1024]{1,0:T(8,128)(2,1)} %param.9, f32[512,1024]{1,0:T(8,128)} %all-reduce.3.cloned.1.call-done, bf16[512,1024]{1,0:T(8,128)(2,1)} %param.10), kind=kOutput, calls=%fused_computation.52 | convolution fusion | flops 7517765632 | bytes 32505856 | tf_op jit(solution)/shard_map/dot_general | solution.py:40
  374.8 0.0 reduce-scatter.5.cloned.1.call-update
  374.8 1.8 fusion.11
  376.7 38.1 %all-reduce.5.cloned.1.call-done = f32[512,128]{0,1:T(8,128)} async-done(((f32[512,128]{0,1:T(8,128)}), f32[512,128]{0,1:T(8,128)}) %all-reduce.5.cloned.1.call-update) | async-done | bytes 262160 | tf_op jit(solution)/shard_map/psum | solution.py:38
  414.8 0.9 slice.52
  415.7 149.3 %reduce-scatter.5.cloned.1.call-done = f32[64,7168]{1,0:T(8,128)} async-done(((f32[512,7168]{1,0:T(8,128)}), f32[64,7168]{1,0:T(8,128)}) %reduce-scatter.5.cloned.1.call-update) | async-done | bytes 1835024 | tf_op jit(solution)/shard_map/reduce_scatter | solution.py:39
  565.0 0.0 copy-start.2
  565.0 0.0 copy-start.4
  565.0 3.8 fusion.14
  568.8 0.1 copy-done.2
  569.0 0.6 copy-done.4
  569.5 1.8 fusion.10
  571.4 0.1 pad_maximum_fusion.2
  571.5 16.9 %psum.23 = f32[64,192]{1,0:T(8,128)S(1)} all-reduce(f32[64,192]{1,0:T(8,128)S(1)} %pad_maximum_fusion.2), channel_id=1, replica_groups=mesh['dp'=8,'tensor'=4] {'tensor'}, use_global_device_ids=true, to_apply=%region_4.0 | all-reduce | flops 12288 | bytes 98304 | tf_op jit(solution)/shard_map/psum | solution.py:55
  588.3 14.8 %all_gather.7 = f32[512,192]{1,0:T(8,128)S(1)} all-gather(f32[64,192]{1,0:T(8,128)S(1)} %psum.23), channel_id=1, replica_groups=mesh['dp'=8,'tensor'=4] {'dp'}, dimensions={0}, use_global_device_ids=true | all-gather | bytes 442368 | tf_op jit(solution)/shard_map/all_gather | solution.py:55
  603.2 1.2 fusion.6
  604.4 1.3 fusion.7
  605.7 0.1 copy.17
  605.8 1.5 fusion.8
  607.3 0.9 pad_maximum_fusion.1
  608.2 0.2 convert_element_type.37
  608.4 0.0 copy-done
  608.4 1.5 fusion.38
  (4 shorter events, 0.0 us)
Async XLA Ops:
  6.5 601.9 %copy-start = (bf16[128,12288]{1,0:T(8,128)(2,1)S(1)}, bf16[128,12288]{1,0:T(8,128)(2,1)}, u32[]{:S(2)}) copy-start(bf16[128,12288]{1,0:T(8,128)(2,1)} %param.13) | copy-start | bytes 9437188
  6.5 190.3 %reduce-scatter.3.cloned.1.call-start = ((), (), s32[]{:S(2)}) async-start(), calls=%async_computation.2 | async-start | bytes 16515072 | tf_op jit(solution)/shard_map/reduce_scatter | solution.py:21
  45.0 228.8 %all-gather.2.cloned.1.call-start = ((), (), s32[]{:S(2)}) async-start(), calls=%async_computation.3 | async-start | bytes 8257536 | tf_op jit(solution)/shard_map/all_gather | solution.py:33
  198.7 1.8 copy-start.1
  201.9 154.6 %all-reduce.3.cloned.1.call-start = ((), (), s32[]{:S(2)}) async-start(), calls=%async_computation.4 | async-start | bytes 4194304 | tf_op jit(solution)/shard_map/psum | solution.py:35
  288.1 0.9 copy-start.3
  288.1 126.7 %all-reduce.5.cloned.1.call-start = ((), (), s32[]{:S(2)}) async-start(), calls=%async_computation.5 | async-start | bytes 524288 | tf_op jit(solution)/shard_map/psum | solution.py:38
  359.7 205.3 %reduce-scatter.5.cloned.1.call-start = ((), (), s32[]{:S(2)}) async-start(), calls=%async_computation.6 | async-start | bytes 16515072 | tf_op jit(solution)/shard_map/reduce_scatter | solution.py:39
  565.0 3.9 copy-start.2
  565.0 4.5 copy-start.4
Sparse Core Ops, SparseCore 0:
  45.1 151.6 reduce-scatter.2
  202.0 71.7 all-gather.1
  288.3 68.2 all-reduce.2
  359.8 54.9 all-reduce.4
  417.0 147.9 reduce-scatter.4
where the time goes:
time: 617 us; the launch traced here: 616 us
  waiting for transfers between devices  477 us (77%)
  matrix products  71 us (12%)
  blocking collectives  31.7 us (5%)
  local copies, waits for them, and re-layouts  18.2 us (3%)
  between operations  13.2 us (2%)
    reduce_scatter x1, waiting for transfers between devices, local(): lax.psum_scatter(both.reshape(n_dp * 2 * rows, width_ff), 'dp', scatter_d...  152 us
    reduce_scatter x1, waiting for transfers between devices, local(): lax.psum_scatter(lax.dot_general(cot, w_down, (((1,), (1,)), ((), ())), p...  149 us
    all_gather x1, waiting for transfers between devices, local(): lax.all_gather(hidden, 'dp', axis=0, tiled=True)  71.8 us
    psum x1, waiting for transfers between devices, local(): out_full = lax.psum(out_part, 'tensor')  65.8 us
    psum x1, waiting for transfers between devices, local(): side = lax.psum(jnp.concatenate([a_in_part, a_out_part], axis=1), 'dp')  38.1 us
    dot_general x1, matrix products, local(): jnp.einsum('td,dkf->ktf', tokens, w_gate_up, preferred_element_type=jnp.f...  24.9 us
    psum x1, blocking collectives, local(): lax.psum(hid_part, 'tensor')  16.9 us
    dot_general x1, matrix products, local(): lax.dot_general(cot, w_down, (((1,), (1,)), ((), ())), preferred_element_...  14.9 us
  transfers between devices with their start and end apart: 5, of which 5 were waited for; matrix products, arithmetic and copies ran while one was open for 3% of the time, Pallas kernels for 0%

commit v1 on v0

--- a/solution.py
+++ b/solution.py
@@ -35,7 +35,7 @@
     out_full = lax.psum(out_part, "tensor")
     cot = (out_full - targets.astype(jnp.float32)).astype(jnp.bfloat16)
     a_out_part = jnp.dot(cot, proj_model[:, RANK:], preferred_element_type=jnp.float32)
-    side = lax.psum(jnp.concatenate([a_in_part, a_out_part], axis=1), "dp")
+    side = jnp.sum(lax.all_gather(jnp.concatenate([a_in_part, a_out_part], axis=1), "dp"), axis=0)
     grad_hidden = lax.psum_scatter(
         lax.dot_general(cot, w_down, (((1,), (1,)), ((), ())), preferred_element_type=jnp.float32),
         "dp",

time: 617 us -> 594 us (0.963)
  waiting for transfers between devices: 477 us -> 448 us
    psum x1 -> x0, waiting for transfers between devices: 38.1 us -> none  [local(): side = lax.psum(jnp.concatenate([a_in_part, a_out_part], axis=1), 'dp')]
    all_gather x0 -> x1, waiting for transfers between devices: none -> 11.6 us  [local(): lax.all_gather(jnp.concatenate([a_in_part, a_out_part], axis=1), 'dp')]
  transfers between devices with their start and end apart: 5 -> 5, of which waited for: 5 -> 5; matrix products, arithmetic and copies ran while one was open for 3% -> 4% of each run, Pallas kernels for 0% -> 0%
where the time goes in v1:
time: 594 us
  waiting for transfers between devices  448 us (75%)
  matrix products  70.7 us (12%)
  blocking collectives  33 us (6%)
  local copies, waits for them, and re-layouts  22.1 us (4%)
  between operations  13.2 us (2%)
  other arithmetic  6.2 us (1%)
    reduce_scatter x1, waiting for transfers between devices, local(): lax.psum_scatter(both.reshape(n_dp * 2 * rows, width_ff), 'dp', scatter_d...  152 us
    reduce_scatter x1, waiting for transfers between devices, local(): lax.psum_scatter(lax.dot_general(cot, w_down, (((1,), (1,)), ((), ())), p...  147 us
    all_gather x1, waiting for transfers between devices, local(): lax.all_gather(hidden, 'dp', axis=0, tiled=True)  71.8 us
    psum x1, waiting for transfers between devices, local(): out_full = lax.psum(out_part, 'tensor')  65.8 us
    dot_general x1, matrix products, local(): jnp.einsum('td,dkf->ktf', tokens, w_gate_up, preferred_element_type=jnp.f...  24.8 us
    psum x1, blocking collectives, local(): lax.psum(hid_part, 'tensor')  18 us
    all_gather x1, blocking collectives, local(): lax.all_gather(lax.psum(hid_part, 'tensor'), 'dp', axis=0, tiled=True)  15 us
    dot_general x1, matrix products, local(): lax.dot_general(cot, w_down, (((1,), (1,)), ((), ())), preferred_element_...  14.9 us
  transfers between devices with their start and end apart: 5, of which 5 were waited for; matrix products, arithmetic and copies ran while one was open for 4% of the time, Pallas kernels for 0%

profile of v1, /device:TPU:0, one launch (start us, length us, event | category | flops | bytes accessed | tf_op | source)
XLA Modules:
  0.0 593.8 jit_solution(8468674766524775205)
XLA Ops:
  6.5 0.0 copy-start
  6.5 0.0 reduce-scatter.3.cloned.1.call-start
  6.5 24.8 %fusion.2 = bf16[2,7168,512]{1,2,0:T(8,128)(2,1)} fusion(bf16[1024,2,7168]{2,1,0:T(2,128)(2,1)} %param.8, bf16[512,1024]{1,0:T(8,128)(2,1)} %param.7), kind=kOutput, calls=%fused_computation.2 | convolution fusion | flops 15039725568 | bytes 45088768 | tf_op jit(solution)/shard_map/td,dkf->ktf/dot_general | solution.py:18
  31.4 13.5 %copy.14 = bf16[8,2,64,7168]{3,2,1,0:T(8,128)(2,1)} copy(bf16[8,2,64,7168]{3,2,0,1:T(8,128)(2,1)} %bitcast.45) | data formatting | bytes 29360128 | tf_op jit(solution)/shard_map/transpose | solution.py:19
  44.9 0.0 reduce-scatter.3.cloned.1.call-update
  44.9 0.0 all-gather.4.cloned.1.call-start
  45.0 151.8 %reduce-scatter.3.cloned.1.call-done = bf16[128,7168]{1,0:T(8,128)(2,1)} async-done(((bf16[1024,7168]{1,0:T(8,128)(2,1)}), bf16[128,7168]{1,0:T(8,128)(2,1)}) %reduce-scatter.3.cloned.1.call-update) | async-done | bytes 1835024 | tf_op jit(solution)/shard_map/reduce_scatter | solution.py:21
  196.8 1.9 convert_element_type.31
  198.6 0.0 copy-start.1
  198.6 1.8 copy-done.1
  200.4 1.4 multiply_convert_fusion.2
  201.9 0.0 all-gather.4.cloned.1.call-update
  201.9 0.0 all-reduce.2.cloned.1.call-start
  201.9 71.8 %all-gather.4.cloned.1.call-done = bf16[512,7168]{1,0:T(8,128)(2,1)} async-done(((bf16[64,7168]{1,0:T(8,128)(2,1)}), bf16[512,7168]{1,0:T(8,128)(2,1)}) %all-gather.4.cloned.1.call-update) | async-done | bytes 7340048 | tf_op jit(solution)/shard_map/all_gather | solution.py:33
  273.8 14.3 %fusion.37 = f32[512,1024]{1,0:T(8,128)} fusion(bf16[512,7168]{1,0:T(8,128)(2,1)} %all-gather.4.cloned.1.call-done, bf16[7168,1024]{1,0:T(8,128)(2,1)} %param.9), kind=kOutput, calls=%fused_computation.54 | convolution fusion | flops 7516192768 | bytes 24117248 | tf_op jit(solution)/shard_map/dot_general | solution.py:32
  288.0 0.0 all-reduce.2.cloned.1.call-update
  288.1 0.0 all-gather.6.cloned.1.call-start
  288.1 0.9 copy-done.3
  289.0 1.7 fusion.27
  290.7 65.8 %all-reduce.2.cloned.1.call-done = f32[512,1024]{1,0:T(8,128)} async-done(((f32[512,1024]{1,0:T(8,128)}), f32[512,1024]{1,0:T(8,128)}) %all-reduce.2.cloned.1.call-update) | async-done | bytes 2097168 | tf_op jit(solution)/shard_map/psum | solution.py:35
  356.5 2.4 fusion.25
  358.9 0.7 pad_maximum_fusion
  359.6 0.0 all-gather.6.cloned.1.call-update
  359.6 0.2 reduce-scatter.5.cloned.1.call-start
  359.8 14.9 %fusion.36 = f32[512,7168]{1,0:T(8,128)} fusion(bf16[7168,1024]{1,0:T(8,128)(2,1)} %param.9, f32[512,1024]{1,0:T(8,128)} %all-reduce.2.cloned.1.call-done, bf16[512,1024]{1,0:T(8,128)(2,1)} %param.10), kind=kOutput, calls=%fused_computation.53 | convolution fusion | flops 7517765632 | bytes 32505856 | tf_op jit(solution)/shard_map/dot_general | solution.py:40
  374.7 0.0 reduce-scatter.5.cloned.1.call-update
  374.8 2.5 fusion.11
  377.2 11.6 %all-gather.6.cloned.1.call-done = f32[4096,128]{0,1:T(8,128)} async-done(((f32[512,128]{0,1:T(8,128)}), f32[4096,128]{0,1:T(8,128)}) %all-gather.6.cloned.1.call-update) | async-done | bytes 2097168 | tf_op jit(solution)/shard_map/all_gather | solution.py:38
  388.9 3.2 copy.23
  392.1 0.5 bitcast_reduce_fusion
  392.7 147.0 %reduce-scatter.5.cloned.1.call-done = f32[64,7168]{1,0:T(8,128)} async-done(((f32[512,7168]{1,0:T(8,128)}), f32[64,7168]{1,0:T(8,128)}) %reduce-scatter.5.cloned.1.call-update) | async-done | bytes 1835024 | tf_op jit(solution)/shard_map/reduce_scatter | solution.py:39
  539.7 3.8 fusion.14
  543.5 0.1 copy-done.2
  543.6 0.6 copy-done.5
  544.2 1.8 fusion.10
  546.0 0.0 copy-done.4
  546.0 0.7 pad_maximum_fusion.2
  546.8 18.0 %psum.15 = f32[64,192]{1,0:T(8,128)} all-reduce(f32[64,192]{1,0:T(8,128)} %pad_maximum_fusion.2), channel_id=1, replica_groups=mesh['dp'=8,'tensor'=4] {'tensor'}, use_global_device_ids=true, to_apply=%region_4.0 | all-reduce | flops 12288 | bytes 98304 | tf_op jit(solution)/shard_map/psum | solution.py:55
  564.7 15.0 %all_gather.15 = f32[512,192]{1,0:T(8,128)S(1)} all-gather(f32[64,192]{1,0:T(8,128)} %psum.15), channel_id=1, replica_groups=mesh['dp'=8,'tensor'=4] {'dp'}, dimensions={0}, use_global_device_ids=true | all-gather | bytes 442368 | tf_op jit(solution)/shard_map/all_gather | solution.py:55
  579.7 1.2 fusion.6
  581.0 1.3 fusion.7
  582.2 0.7 slice.55
  583.0 1.1 copy.17
  584.0 0.6 fusion.8
  584.6 0.9 pad_maximum_fusion.1
  585.6 0.2 convert_element_type.37
  585.7 0.0 copy-done
  585.7 1.5 fusion.38
  (8 shorter events, 0.0 us)
Async XLA Ops:
  6.5 579.2 %copy-start = (bf16[128,12288]{1,0:T(8,128)(2,1)S(1)}, bf16[128,12288]{1,0:T(8,128)(2,1)}, u32[]{:S(2)}) copy-start(bf16[128,12288]{1,0:T(8,128)(2,1)} %param.13) | copy-start | bytes 9437188
  6.5 190.2 %reduce-scatter.3.cloned.1.call-start = ((), (), s32[]{:S(2)}) async-start(), calls=%async_computation.2 | async-start | bytes 16515072 | tf_op jit(solution)/shard_map/reduce_scatter | solution.py:21
  44.9 228.9 %all-gather.4.cloned.1.call-start = ((), (), s32[]{:S(2)}) async-start(), calls=%async_computation.3 | async-start | bytes 8257536 | tf_op jit(solution)/shard_map/all_gather | solution.py:33
  198.6 1.8 copy-start.1
  201.9 154.6 %all-reduce.2.cloned.1.call-start = ((), (), s32[]{:S(2)}) async-start(), calls=%async_computation.4 | async-start | bytes 4194304 | tf_op jit(solution)/shard_map/psum | solution.py:35
  288.0 0.9 copy-start.3
  288.1 100.8 %all-gather.6.cloned.1.call-start = ((), (), s32[]{:S(2)}) async-start(), calls=%async_computation.6 | async-start | bytes 2359296 | tf_op jit(solution)/shard_map/all_gather | solution.py:38
  359.6 180.1 %reduce-scatter.5.cloned.1.call-start = ((), (), s32[]{:S(2)}) async-start(), calls=%async_computation.5 | async-start | bytes 16515072 | tf_op jit(solution)/shard_map/reduce_scatter | solution.py:39
  539.7 3.9 copy-start.2
  539.7 4.5 copy-start.5
  544.2 1.8 copy-start.4
Sparse Core Ops, SparseCore 0:
  45.0 151.6 reduce-scatter.2
  202.0 71.7 all-gather.3
  288.2 68.2 all-reduce.1
  359.7 29.1 all-gather.5
  391.1 148.4 reduce-scatter.4
